TPU v7x, 256 devices: a whole 4x4x8 slice. The times are simulated.
256 devices in a mesh: pos: 16 (over x_hi, z), exp: 16 (over y, x_lo, core).
Axes of the slice: x: 4 (x_hi: 2, x_lo: 2; x = x_hi * 2 + x_lo), y: 4, z: 8, core: 2. Of those that a mesh axis runs over, the one named last changes fastest.
Arguments:
- patches: bfloat16 [65536, 4, 256], P(('pos', 'exp')), may hold values from -6 to 6
- conv_weight: bfloat16 [3, 256, 2048], replicated, may hold values from -0.21875 to 0.21875
- phi: bfloat16 [2048, 128], replicated, may hold values from -40 to 40, as said below
- w_in: bfloat16 [16, 2048, 8192], P('exp', None, 'pos'), may hold values from -0.125 to 0.125
- w_out: bfloat16 [16, 8192, 2048], P('exp', 'pos'), may hold values from -0.0625 to 0.0625
Outputs:
- mixed: bfloat16 [65536, 4, 2048], P(('pos', 'exp'))
Inputs may be any that keep to these rules, and one draw needn't show every extreme that they name: phi is real-valued.
All inputs are finite; a program needn't handle non-finite values.
Results may differ from a plain program's by a relative error of at most 0.019.
The roundings to bfloat16 on the way count: a program that leaves them out, or rounds other values in their place, can miss the bound.
Values may be sent and summed in bfloat16 or wider, within the bound.
No kernel may reach another device: no remote copies, remote signals or barrier semaphores. Data moves between devices by JAX's collectives and lax.ppermute only.
A program may use at most 128 MiB of HBM per device.

v0:
```python
import jax
import jax.numpy as jnp
from jax import lax
from jax.sharding import PartitionSpec as P

D = 2048
SLOTS_PER = 8


def with_halo(array, sides, width):
    for axis, dim in sides:
        count, length = (lax.axis_size(axis), array.shape[dim])
        up = [(i, (i + 1) % count) for i in range(count - 1)]
        down = [(j, i) for i, j in up]
        last = lax.slice_in_dim(array, length - width, length, axis=dim)
        initial = lax.slice_in_dim(array, 0, width, axis=dim)
        before = lax.ppermute(last, axis, up)
        after = lax.ppermute(initial, axis, down)
        array = jnp.concatenate([before, array, after], axis=dim)
    return array


def butterfly_sum(value, axis):
    count = lax.axis_size(axis)
    step = 1
    while step < count:
        pairs = [(i, i ^ step) for i in range(count)]
        value = value + lax.ppermute(value, axis, pairs)
        step *= 2
    return value


def gather_rows(row, axes):
    count = lax.axis_size(axes)
    tiled = jnp.broadcast_to(row[None, :], (count, row.shape[0]))
    return lax.all_to_all(tiled, axes, 0, 0, tiled=True)


def per_device(patches, conv_weight, phi, w_in, w_out):
    channels, periods, samples = patches.shape
    every = ("pos", "exp")
    padded = with_halo(patches, ((every, 0),), 1)
    running = jnp.zeros((channels * periods, D), jnp.float32)
    for offset in range(3):
        window = padded[offset : offset + channels].reshape(channels * periods, samples)
        running = running + jnp.dot(window, conv_weight[offset], preferred_element_type=jnp.float32)
    flat = running.astype(jnp.bfloat16)
    logits = jnp.dot(flat, phi, preferred_element_type=jnp.float32)
    slots = logits.shape[1]
    local_peak = jnp.max(logits, axis=0)
    local_total = jnp.sum(jnp.exp(logits - local_peak), axis=0)
    stats = gather_rows(jnp.concatenate([local_peak, local_total]), every)
    peaks, totals = (stats[:, :slots], stats[:, slots:])
    column_peak = jnp.max(peaks, axis=0)
    column_total = jnp.sum(totals * jnp.exp(peaks - column_peak), axis=0)
    raw_weights = jnp.exp(logits - column_peak)
    dispatch = (raw_weights / column_total).astype(jnp.bfloat16)
    every_slot = lax.dot_general(
        dispatch, flat, (((0,), (0,)), ((), ())), preferred_element_type=jnp.float32
    )
    groups = lax.axis_size("exp")
    mine = lax.all_to_all(every_slot, "exp", 0, 0, tiled=True)
    owned = jnp.sum(mine.reshape(groups, SLOTS_PER, D), axis=0)
    slot_in = butterfly_sum(owned, "pos").astype(jnp.bfloat16)
    hidden = jax.nn.gelu(
        jnp.dot(slot_in, w_in[0], preferred_element_type=jnp.float32), approximate=True
    ).astype(jnp.bfloat16)
    expert_term = jnp.dot(hidden, w_out[0], preferred_element_type=jnp.float32)
    slot_out = butterfly_sum(expert_term, "pos").astype(jnp.bfloat16)
    row_peak = jnp.max(logits, axis=1, keepdims=True)
    row_weights = jnp.exp(logits - row_peak)
    combine = (row_weights / jnp.sum(row_weights, axis=1, keepdims=True)).astype(jnp.bfloat16)
    mixed = jnp.dot(
        combine,
        lax.all_gather(slot_out, "exp", axis=0, tiled=True),
        preferred_element_type=jnp.float32,
    )
    return mixed.astype(jnp.bfloat16).reshape(channels, periods, D)


def solution(mesh):
    in_specs = (
        P(("pos", "exp"), None, None),
        P(),
        P(),
        P("exp", None, "pos"),
        P("exp", "pos", None),
    )
    out_specs = P(("pos", "exp"), None, None)
    return jax.shard_map(
        per_device, mesh=mesh, in_specs=in_specs, out_specs=out_specs, check_vma=False
    )
```

profile of v0, /device:TPU:1, one launch (start us, length us, event | category | flops | bytes accessed | tf_op | source)
XLA Modules:
  0.0 161.6 jit_solution(5333478168599324480)
XLA Ops:
  0.0 0.0 copy-start
  0.0 0.9 fusion.44
  0.9 5.1 %collective-permute-start.1 = (bf16[1,4,256]{2,1,0:T(4,128)(2,1)S(1)}, bf16[1,4,256]{2,1,0:T(4,128)(2,1)S(1)}, u32[]{:S(2)}, u32[]{:S(2)}) collective-permute-start(bf16[1,4,256]{2,1,0:T(4,128)(2,1)S(1)} %get-tuple-element.11), channel_id=1, source_target_pairs={{1,0},{2,1},{3,2},{4,3},{5,4},{6,5},{7,6},{8,7},{9,8},{10,9},{11,1... | collective-permute-start | bytes 6152 | tf_op jit(solution)/shard_map/ppermute | solution.py:18
  6.0 1.9 %collective-permute-start = (bf16[1,4,256]{2,1,0:T(4,128)(2,1)S(1)}, bf16[1,4,256]{2,1,0:T(4,128)(2,1)S(1)}, u32[]{:S(2)}, u32[]{:S(2)}) collective-permute-start(bf16[1,4,256]{2,1,0:T(4,128)(2,1)S(1)} %get-tuple-element.12), channel_id=1, source_target_pairs={{0,1},{1,2},{2,3},{3,4},{4,5},{5,6},{6,7},{7,8},{8,9},{9,10},{10,1... | collective-permute-start | bytes 6152 | tf_op jit(solution)/shard_map/ppermute | solution.py:17
  7.9 1.2 reshape.28
  9.1 0.0 copy-start.2
  9.1 5.8 %fusion.8 = f32[1024,2048]{1,0:T(8,128)} fusion(bf16[1024,256]{1,0:T(8,128)(2,1)S(1)} %reshape.28, bf16[3,256,2048]{2,1,0:T(8,128)(2,1)} %param.6), kind=kOutput, calls=%fused_computation.9 | convolution fusion | flops 1073741824 | bytes 9961472 | tf_op jit(solution)/shard_map/dot_general | solution.py:46
  14.8 0.0 collective-permute-done.1
  14.8 0.0 collective-permute-done
  14.8 0.0 copy-done.2
  14.8 1.2 pad_maximum_fusion
  16.0 0.1 reshape.29
  16.1 1.2 reshape.27
  17.3 0.0 copy-start.1
  17.3 2.6 %fusion.10 = f32[1024,2048]{1,0:T(8,128)S(1)} fusion(bf16[1024,256]{1,0:T(8,128)(2,1)S(1)} %reshape.27, bf16[3,256,2048]{2,1,0:T(8,128)(2,1)} %param.6), kind=kOutput, calls=%fused_computation.11 | convolution fusion | flops 1073741824 | bytes 9961472 | tf_op jit(solution)/shard_map/dot_general | solution.py:46
  20.0 1.0 copy-done.1
  21.0 0.0 copy-start.3
  21.0 2.7 %add_convert_fusion = bf16[1024,2048]{1,0:T(8,128)(2,1)S(1)} fusion(f32[1024,2048]{1,0:T(8,128)S(1)} %fusion.10, f32[1024,2048]{1,0:T(8,128)S(1)} %copy-done.1, bf16[1024,256]{1,0:T(8,128)(2,1)S(1)} %reshape.29, bf16[3,256,2048]{2,1,0:T(8,128)(2,1)} %param.6), kind=kOutput, calls=%fused_computation | convolution fusion | flops 1080033280 | bytes 22544384 | tf_op jit(solution)/shard_map/dot_general | solution.py:46
  23.7 0.0 copy-done.3
  23.8 1.3 fusion.43
  25.1 0.4 fusion.15
  25.5 0.1 broadcast_in_dim.2
  25.6 31.6 %all_to_all.18 = f32[256,1,256]{2,1,0:T(1,128)S(1)} all-to-all(f32[256,1,256]{2,1,0:T(1,128)S(1)} %broadcast_in_dim.2), channel_id=1, replica_groups=mesh['pos'=16,'exp'=16] {'pos','exp'}, dimensions={0} | all-to-all | bytes 524288 | tf_op jit(solution)/shard_map/all_to_all | solution.py:36
  57.3 0.1 fusion.20
  57.4 0.8 convolution_bitcast_fusion
  58.2 18.9 %all_to_all.19 = f32[16,8,2048]{2,1,0:T(8,128)} all-to-all(f32[16,8,2048]{2,1,0:T(8,128)S(1)} %convolution_bitcast_fusion), channel_id=1, replica_groups=mesh['pos'=16,'exp'=16] {'exp'}, dimensions={0} | all-to-all | bytes 2097152 | tf_op jit(solution)/shard_map/all_to_all | solution.py:62
  77.1 1.3 reduce_sum.39
  78.4 0.9 collective-permute-start.2
  79.2 2.3 %collective-permute-done.2 = f32[8,2048]{1,0:T(8,128)S(1)} collective-permute-done((f32[8,2048]{1,0:T(8,128)S(1)}, f32[8,2048]{1,0:T(8,128)S(1)}, u32[]{:S(2)}, u32[]{:S(2)}) %collective-permute-start.2) | collective-permute-done | bytes 65568 | tf_op jit(solution)/shard_map/ppermute | solution.py:28
  81.6 0.6 collective-permute-start.3
  82.2 4.2 %collective-permute-done.3 = f32[8,2048]{1,0:T(8,128)S(1)} collective-permute-done((f32[8,2048]{1,0:T(8,128)S(1)}, f32[8,2048]{1,0:T(8,128)S(1)}, u32[]{:S(2)}, u32[]{:S(2)}) %collective-permute-start.3) | collective-permute-done | bytes 65568 | tf_op jit(solution)/shard_map/ppermute | solution.py:28
  86.4 1.1 collective-permute-start.4
  87.5 6.3 %collective-permute-done.4 = f32[8,2048]{1,0:T(8,128)S(1)} collective-permute-done((f32[8,2048]{1,0:T(8,128)S(1)}, f32[8,2048]{1,0:T(8,128)S(1)}, u32[]{:S(2)}, u32[]{:S(2)}) %collective-permute-start.4) | collective-permute-done | bytes 65568 | tf_op jit(solution)/shard_map/ppermute | solution.py:28
  93.7 1.3 collective-permute-start.5
  95.0 3.4 %collective-permute-done.5 = f32[8,2048]{1,0:T(8,128)S(1)} collective-permute-done((f32[8,2048]{1,0:T(8,128)S(1)}, f32[8,2048]{1,0:T(8,128)S(1)}, u32[]{:S(2)}, u32[]{:S(2)}) %collective-permute-start.5) | collective-permute-done | bytes 65568 | tf_op jit(solution)/shard_map/ppermute | solution.py:28
  98.4 0.0 copy-done
  98.4 2.3 %fusion = f32[8,2048]{1,0:T(8,128)S(1)} fusion(bf16[1,512,2048]{2,1,0:T(8,128)(2,1)S(1)} %copy-done, bf16[1,2048,512]{2,1,0:T(8,128)(2,1)} %param.8, f32[8,2048]{1,0:T(8,128)S(1)} %add.43, f32[8,2048]{1,0:T(8,128)S(1)} %collective-permute-done.5), kind=kOutput, calls=%fused_computation.3 | convolution fusion | flops 33624064 | bytes 4390912 | tf_op jit(solution)/shard_map/dot_general | solution.py:68
  100.8 0.2 collective-permute-start.6
  101.0 3.1 %collective-permute-done.6 = f32[8,2048]{1,0:T(8,128)S(1)} collective-permute-done((f32[8,2048]{1,0:T(8,128)S(1)}, f32[8,2048]{1,0:T(8,128)S(1)}, u32[]{:S(2)}, u32[]{:S(2)}) %collective-permute-start.6) | collective-permute-done | bytes 65568 | tf_op jit(solution)/shard_map/ppermute | solution.py:28
  104.1 0.2 collective-permute-start.7
  104.2 4.4 %collective-permute-done.7 = f32[8,2048]{1,0:T(8,128)S(1)} collective-permute-done((f32[8,2048]{1,0:T(8,128)S(1)}, f32[8,2048]{1,0:T(8,128)S(1)}, u32[]{:S(2)}, u32[]{:S(2)}) %collective-permute-start.7) | collective-permute-done | bytes 65568 | tf_op jit(solution)/shard_map/ppermute | solution.py:28
  108.6 1.1 collective-permute-start.8
  109.7 6.6 %collective-permute-done.8 = f32[8,2048]{1,0:T(8,128)S(1)} collective-permute-done((f32[8,2048]{1,0:T(8,128)S(1)}, f32[8,2048]{1,0:T(8,128)S(1)}, u32[]{:S(2)}, u32[]{:S(2)}) %collective-permute-start.8) | collective-permute-done | bytes 65568 | tf_op jit(solution)/shard_map/ppermute | solution.py:28
  116.3 1.2 collective-permute-start.9
  117.5 3.6 %collective-permute-done.9 = f32[8,2048]{1,0:T(8,128)S(1)} collective-permute-done((f32[8,2048]{1,0:T(8,128)S(1)}, f32[8,2048]{1,0:T(8,128)S(1)}, u32[]{:S(2)}, u32[]{:S(2)}) %collective-permute-start.9) | collective-permute-done | bytes 65568 | tf_op jit(solution)/shard_map/ppermute | solution.py:28
  121.0 30.1 %all_gather.3 = bf16[128,2048]{1,0:T(8,128)(2,1)S(1)} all-gather(bf16[8,2048]{1,0:T(8,128)(2,1)S(1)} %add_convert_fusion.1), channel_id=1, replica_groups=mesh['pos'=16,'exp'=16] {'exp'}, dimensions={0}, use_global_device_ids=true | all-gather | bytes 557056 | tf_op jit(solution)/shard_map/all_gather | solution.py:75
  151.2 3.2 %convolution_convert_fusion = bf16[1024,2048]{1,0:T(8,128)(2,1)} fusion(bf16[128,2048]{1,0:T(8,128)(2,1)S(1)} %all_gather.3, f32[1024,128]{1,0:T(8,128)S(1)} %get-tuple-element.13, f32[1024]{0:T(1024)S(1)} %get-tuple-element.5, f32[1024]{0:T(1024)S(1)} %get-tuple-element.7), kind=kOutput, calls=%fused_computation.1 | convolution fusion | flops 539361280 | bytes 5251072 | tf_op jit(solution)/shard_map/dot_general | solution.py:73
  154.4 7.2 %reshape.30 = bf16[256,4,2048]{2,1,0:T(4,128)(2,1)} reshape(bf16[1024,2048]{1,0:T(8,128)(2,1)} %convolution_convert_fusion) | data formatting | bytes 8388608 | tf_op jit(solution)/shard_map/reshape | solution.py:78
  (10 shorter events, 0.1 us)
Async XLA Ops:
  0.0 98.4 %copy-start = (bf16[1,512,2048]{2,1,0:T(8,128)(2,1)S(1)}, bf16[1,512,2048]{2,1,0:T(8,128)(2,1)}, u32[]{:S(2)}) copy-start(bf16[1,512,2048]{2,1,0:T(8,128)(2,1)} %param.9) | copy-start | bytes 6291460
  0.9 14.0 %collective-permute-start.1 = (bf16[1,4,256]{2,1,0:T(4,128)(2,1)S(1)}, bf16[1,4,256]{2,1,0:T(4,128)(2,1)S(1)}, u32[]{:S(2)}, u32[]{:S(2)}) collective-permute-start(bf16[1,4,256]{2,1,0:T(4,128)(2,1)S(1)} %get-tuple-element.11), channel_id=1, source_target_pairs={{1,0},{2,1},{3,2},{4,3},{5,4},{6,5},{7,6},{8,7},{9,8},{10,9},{11,1... | collective-permute-start | bytes 6152 | tf_op jit(solution)/shard_map/ppermute | solution.py:18
  6.0 8.9 %collective-permute-start = (bf16[1,4,256]{2,1,0:T(4,128)(2,1)S(1)}, bf16[1,4,256]{2,1,0:T(4,128)(2,1)S(1)}, u32[]{:S(2)}, u32[]{:S(2)}) collective-permute-start(bf16[1,4,256]{2,1,0:T(4,128)(2,1)S(1)} %get-tuple-element.12), channel_id=1, source_target_pairs={{0,1},{1,2},{2,3},{3,4},{4,5},{5,6},{6,7},{7,8},{8,9},{9,10},{10,1... | collective-permute-start | bytes 6152 | tf_op jit(solution)/shard_map/ppermute | solution.py:17
  9.1 5.8 %copy-start.2 = (bf16[256,4,256]{2,1,0:T(4,128)(2,1)S(1)}, bf16[256,4,256]{2,1,0:T(4,128)(2,1)}, u32[]{:S(2)}) copy-start(bf16[256,4,256]{2,1,0:T(4,128)(2,1)} %param.5) | copy-start | bytes 1572868
  17.3 3.7 %copy-start.1 = (f32[1024,2048]{1,0:T(8,128)S(1)}, f32[1024,2048]{1,0:T(8,128)}, u32[]{:S(2)}) copy-start(f32[1024,2048]{1,0:T(8,128)} %fusion.8) | copy-start | bytes 25165828
  21.0 2.7 %copy-start.3 = (bf16[2048,128]{1,0:T(8,128)(2,1)S(1)}, bf16[2048,128]{1,0:T(8,128)(2,1)}, u32[]{:S(2)}) copy-start(bf16[2048,128]{1,0:T(8,128)(2,1)} %param.7) | copy-start | bytes 1572868
  78.4 3.2 %collective-permute-start.2 = (f32[8,2048]{1,0:T(8,128)S(1)}, f32[8,2048]{1,0:T(8,128)S(1)}, u32[]{:S(2)}, u32[]{:S(2)}) collective-permute-start(f32[8,2048]{1,0:T(8,128)S(1)} %reduce_sum.39), channel_id=1, source_target_pairs={{0,16},{16,0},{32,48},{48,32},{64,80},{80,64},{96,112},{112,96},{1... | collective-permute-start | bytes 196616 | tf_op jit(solution)/shard_map/ppermute | solution.py:28
  81.6 4.8 %collective-permute-start.3 = (f32[8,2048]{1,0:T(8,128)S(1)}, f32[8,2048]{1,0:T(8,128)S(1)}, u32[]{:S(2)}, u32[]{:S(2)}) collective-permute-start(f32[8,2048]{1,0:T(8,128)S(1)} %add.41), channel_id=1, source_target_pairs={{0,32},{16,48},{32,0},{48,16},{64,96},{80,112},{96,64},{112,80},{1... | collective-permute-start | bytes 196616 | tf_op jit(solution)/shard_map/ppermute | solution.py:28
  86.4 7.3 %collective-permute-start.4 = (f32[8,2048]{1,0:T(8,128)S(1)}, f32[8,2048]{1,0:T(8,128)S(1)}, u32[]{:S(2)}, u32[]{:S(2)}) collective-permute-start(f32[8,2048]{1,0:T(8,128)S(1)} %add.42), channel_id=1, source_target_pairs={{0,64},{16,80},{32,96},{48,112},{64,0},{80,16},{96,32},{112,48},{1... | collective-permute-start | bytes 196616 | tf_op jit(solution)/shard_map/ppermute | solution.py:28
  93.7 4.7 %collective-permute-start.5 = (f32[8,2048]{1,0:T(8,128)S(1)}, f32[8,2048]{1,0:T(8,128)S(1)}, u32[]{:S(2)}, u32[]{:S(2)}) collective-permute-start(f32[8,2048]{1,0:T(8,128)S(1)} %add.43), channel_id=1, source_target_pairs={{0,128},{16,144},{32,160},{48,176},{64,192},{80,208},{96,224},{112... | collective-permute-start | bytes 196616 | tf_op jit(solution)/shard_map/ppermute | solution.py:28
  100.8 3.3 %collective-permute-start.6 = (f32[8,2048]{1,0:T(8,128)S(1)}, f32[8,2048]{1,0:T(8,128)S(1)}, u32[]{:S(2)}, u32[]{:S(2)}) collective-permute-start(f32[8,2048]{1,0:T(8,128)S(1)} %fusion), channel_id=1, source_target_pairs={{0,16},{16,0},{32,48},{48,32},{64,80},{80,64},{96,112},{112,96},{1... | collective-permute-start | bytes 196616 | tf_op jit(solution)/shard_map/ppermute | solution.py:28
  104.1 4.5 %collective-permute-start.7 = (f32[8,2048]{1,0:T(8,128)S(1)}, f32[8,2048]{1,0:T(8,128)S(1)}, u32[]{:S(2)}, u32[]{:S(2)}) collective-permute-start(f32[8,2048]{1,0:T(8,128)S(1)} %add.48), channel_id=1, source_target_pairs={{0,32},{16,48},{32,0},{48,16},{64,96},{80,112},{96,64},{112,80},{1... | collective-permute-start | bytes 196616 | tf_op jit(solution)/shard_map/ppermute | solution.py:28
  108.6 7.7 %collective-permute-start.8 = (f32[8,2048]{1,0:T(8,128)S(1)}, f32[8,2048]{1,0:T(8,128)S(1)}, u32[]{:S(2)}, u32[]{:S(2)}) collective-permute-start(f32[8,2048]{1,0:T(8,128)S(1)} %add.49), channel_id=1, source_target_pairs={{0,64},{16,80},{32,96},{48,112},{64,0},{80,16},{96,32},{112,48},{1... | collective-permute-start | bytes 196616 | tf_op jit(solution)/shard_map/ppermute | solution.py:28
  116.3 4.7 %collective-permute-start.9 = (f32[8,2048]{1,0:T(8,128)S(1)}, f32[8,2048]{1,0:T(8,128)S(1)}, u32[]{:S(2)}, u32[]{:S(2)}) collective-permute-start(f32[8,2048]{1,0:T(8,128)S(1)} %add.50), channel_id=1, source_target_pairs={{0,128},{16,144},{32,160},{48,176},{64,192},{80,208},{96,224},{112... | collective-permute-start | bytes 196616 | tf_op jit(solution)/shard_map/ppermute | solution.py:28
where the time goes:
time: 162 us
  blocking collectives  80.7 us (50%)
  waiting for transfers between devices  33.8 us (21%)
  matrix products  18.8 us (12%)
  starting transfers between devices  13.4 us (8%)
  local copies, waits for them, and re-layouts  11.7 us (7%)
  other arithmetic  3 us (2%)
    ppermute x8, waiting for transfers between devices, butterfly_sum(): value = value + lax.ppermute(value, axis, pairs)  33.8 us
    all_to_all x1, blocking collectives, gather_rows(): return lax.all_to_all(tiled, axes, 0, 0, tiled=True)  31.6 us
    all_gather x1, blocking collectives, per_device(): lax.all_gather(slot_out, 'exp', axis=0, tiled=True)  30.1 us
    all_to_all x1, blocking collectives, per_device(): mine = lax.all_to_all(every_slot, 'exp', 0, 0, tiled=True)  18.9 us
    dot_general x3, matrix products, per_device(): jnp.dot(window, conv_weight[offset], preferred_element_type=jnp.float32)  11.1 us
    reshape x1, local copies, waits for them, and re-layouts, per_device(): return mixed.astype(jnp.bfloat16).reshape(channels, periods, D)  7.16 us
    ppermute x8, starting transfers between devices, butterfly_sum(): value = value + lax.ppermute(value, axis, pairs)  6.42 us
    ppermute x1, starting transfers between devices, with_halo(): after = lax.ppermute(initial, axis, down)  5.1 us
  transfers between devices with their start and end apart: 10, of which 8 were waited for; matrix products, arithmetic and copies ran while one was open for 4% of the time, Pallas kernels for 0%

commit v1 on v0

--- a/solution.py
+++ b/solution.py
@@ -5,6 +5,19 @@
 
 D = 2048
 SLOTS_PER = 8
+
+
+def clear_patches(target, mesh_ax="exp"):
+    reached = jnp.concatenate(
+        jax.lax.all_to_all(
+            jnp.stack(tuple((target for _ in range(jax.lax.axis_size(mesh_ax)))), axis=0),
+            mesh_ax,
+            0,
+            0,
+        ),
+        axis=0,
+    )
+    return reached
 
 
 def with_halo(array, sides, width):
@@ -70,11 +83,7 @@
     row_peak = jnp.max(logits, axis=1, keepdims=True)
     row_weights = jnp.exp(logits - row_peak)
     combine = (row_weights / jnp.sum(row_weights, axis=1, keepdims=True)).astype(jnp.bfloat16)
-    mixed = jnp.dot(
-        combine,
-        lax.all_gather(slot_out, "exp", axis=0, tiled=True),
-        preferred_element_type=jnp.float32,
-    )
+    mixed = jnp.dot(combine, clear_patches(slot_out), preferred_element_type=jnp.float32)
     return mixed.astype(jnp.bfloat16).reshape(channels, periods, D)
 
 

time: 162 us -> 155 us (0.957)
  blocking collectives: 80.7 us -> 73.4 us
    all_gather x1 -> x0, blocking collectives: 30.1 us -> none  [per_device(): lax.all_gather(slot_out, 'exp', axis=0, tiled=True)]
    all_to_all x0 -> x1, blocking collectives: none -> 22.9 us  [clear_patches(): jax.lax.all_to_all(jnp.stack(tuple((target for _ in range(jax.lax.axis_si...]
where the time goes in v1:
time: 155 us; the launch traced here: 154 us
  blocking collectives  73.4 us (47%)
  waiting for transfers between devices  33.8 us (22%)
  matrix products  18.8 us (12%)
  starting transfers between devices  13.4 us (9%)
  local copies, waits for them, and re-layouts  11.7 us (8%)
  other arithmetic  3 us (2%)
    ppermute x8, waiting for transfers between devices, butterfly_sum(): value = value + lax.ppermute(value, axis, pairs)  33.8 us
    all_to_all x1, blocking collectives, gather_rows(): return lax.all_to_all(tiled, axes, 0, 0, tiled=True)  31.6 us
    all_to_all x1, blocking collectives, clear_patches(): jax.lax.all_to_all(jnp.stack(tuple((target for _ in range(jax.lax.axis_si...  22.9 us
    all_to_all x1, blocking collectives, per_device(): mine = lax.all_to_all(every_slot, 'exp', 0, 0, tiled=True)  18.9 us
    dot_general x3, matrix products, per_device(): jnp.dot(window, conv_weight[offset], preferred_element_type=jnp.float32)  11.1 us
    reshape x1, local copies, waits for them, and re-layouts, per_device(): return mixed.astype(jnp.bfloat16).reshape(channels, periods, D)  7.16 us
    ppermute x8, starting transfers between devices, butterfly_sum(): value = value + lax.ppermute(value, axis, pairs)  6.42 us
    ppermute x1, starting transfers between devices, with_halo(): after = lax.ppermute(initial, axis, down)  5.1 us
  transfers between devices with their start and end apart: 10, of which 8 were waited for; matrix products, arithmetic and copies ran while one was open for 4% of the time, Pallas kernels for 0%

profile of v1, /device:TPU:1, one launch (start us, length us, event | category | flops | bytes accessed | tf_op | source)
XLA Modules:
  0.0 154.4 jit_solution(15296549741433625101)
XLA Ops:
  0.0 0.0 copy-start
  0.0 0.9 fusion.45
  0.9 5.1 %collective-permute-start.1 = (bf16[1,4,256]{2,1,0:T(4,128)(2,1)S(1)}, bf16[1,4,256]{2,1,0:T(4,128)(2,1)S(1)}, u32[]{:S(2)}, u32[]{:S(2)}) collective-permute-start(bf16[1,4,256]{2,1,0:T(4,128)(2,1)S(1)} %get-tuple-element.11), channel_id=1, source_target_pairs={{1,0},{2,1},{3,2},{4,3},{5,4},{6,5},{7,6},{8,7},{9,8},{10,9},{11,1... | collective-permute-start | bytes 6152 | tf_op jit(solution)/shard_map/ppermute | solution.py:31
  6.0 1.9 %collective-permute-start = (bf16[1,4,256]{2,1,0:T(4,128)(2,1)S(1)}, bf16[1,4,256]{2,1,0:T(4,128)(2,1)S(1)}, u32[]{:S(2)}, u32[]{:S(2)}) collective-permute-start(bf16[1,4,256]{2,1,0:T(4,128)(2,1)S(1)} %get-tuple-element.12), channel_id=1, source_target_pairs={{0,1},{1,2},{2,3},{3,4},{4,5},{5,6},{6,7},{7,8},{8,9},{9,10},{10,1... | collective-permute-start | bytes 6152 | tf_op jit(solution)/shard_map/ppermute | solution.py:30
  7.9 1.2 reshape.33
  9.1 0.0 copy-start.2
  9.1 5.8 %fusion.8 = f32[1024,2048]{1,0:T(8,128)} fusion(bf16[1024,256]{1,0:T(8,128)(2,1)S(1)} %reshape.33, bf16[3,256,2048]{2,1,0:T(8,128)(2,1)} %param.6), kind=kOutput, calls=%fused_computation.9 | convolution fusion | flops 1073741824 | bytes 9961472 | tf_op jit(solution)/shard_map/dot_general | solution.py:59
  14.8 0.0 collective-permute-done.1
  14.8 0.0 collective-permute-done
  14.8 0.0 copy-done.2
  14.8 1.2 pad_maximum_fusion
  16.0 0.1 reshape.34
  16.1 1.2 reshape.32
  17.3 0.0 copy-start.1
  17.3 2.6 %fusion.10 = f32[1024,2048]{1,0:T(8,128)S(1)} fusion(bf16[1024,256]{1,0:T(8,128)(2,1)S(1)} %reshape.32, bf16[3,256,2048]{2,1,0:T(8,128)(2,1)} %param.6), kind=kOutput, calls=%fused_computation.11 | convolution fusion | flops 1073741824 | bytes 9961472 | tf_op jit(solution)/shard_map/dot_general | solution.py:59
  20.0 1.0 copy-done.1
  21.0 0.0 copy-start.3
  21.0 2.7 %add_convert_fusion = bf16[1024,2048]{1,0:T(8,128)(2,1)S(1)} fusion(f32[1024,2048]{1,0:T(8,128)S(1)} %fusion.10, f32[1024,2048]{1,0:T(8,128)S(1)} %copy-done.1, bf16[1024,256]{1,0:T(8,128)(2,1)S(1)} %reshape.34, bf16[3,256,2048]{2,1,0:T(8,128)(2,1)} %param.6), kind=kOutput, calls=%fused_computation | convolution fusion | flops 1080033280 | bytes 22544384 | tf_op jit(solution)/shard_map/dot_general | solution.py:59
  23.7 0.0 copy-done.3
  23.8 1.3 fusion.44
  25.1 0.4 fusion.16
  25.5 0.1 broadcast_in_dim.2
  25.6 31.6 %all_to_all.23 = f32[256,1,256]{2,1,0:T(1,128)S(1)} all-to-all(f32[256,1,256]{2,1,0:T(1,128)S(1)} %broadcast_in_dim.2), channel_id=1, replica_groups=mesh['pos'=16,'exp'=16] {'pos','exp'}, dimensions={0} | all-to-all | bytes 524288 | tf_op jit(solution)/shard_map/all_to_all | solution.py:49
  57.3 0.1 fusion.21
  57.4 0.8 convolution_bitcast_fusion
  58.2 18.9 %all_to_all.24 = f32[16,8,2048]{2,1,0:T(8,128)} all-to-all(f32[16,8,2048]{2,1,0:T(8,128)S(1)} %convolution_bitcast_fusion), channel_id=1, replica_groups=mesh['pos'=16,'exp'=16] {'exp'}, dimensions={0} | all-to-all | bytes 2097152 | tf_op jit(solution)/shard_map/all_to_all | solution.py:75
  77.1 1.3 reduce_sum.39
  78.4 0.9 collective-permute-start.2
  79.2 2.3 %collective-permute-done.2 = f32[8,2048]{1,0:T(8,128)S(1)} collective-permute-done((f32[8,2048]{1,0:T(8,128)S(1)}, f32[8,2048]{1,0:T(8,128)S(1)}, u32[]{:S(2)}, u32[]{:S(2)}) %collective-permute-start.2) | collective-permute-done | bytes 65568 | tf_op jit(solution)/shard_map/ppermute | solution.py:41
  81.6 0.6 collective-permute-start.3
  82.2 4.2 %collective-permute-done.3 = f32[8,2048]{1,0:T(8,128)S(1)} collective-permute-done((f32[8,2048]{1,0:T(8,128)S(1)}, f32[8,2048]{1,0:T(8,128)S(1)}, u32[]{:S(2)}, u32[]{:S(2)}) %collective-permute-start.3) | collective-permute-done | bytes 65568 | tf_op jit(solution)/shard_map/ppermute | solution.py:41
  86.4 1.1 collective-permute-start.4
  87.5 6.3 %collective-permute-done.4 = f32[8,2048]{1,0:T(8,128)S(1)} collective-permute-done((f32[8,2048]{1,0:T(8,128)S(1)}, f32[8,2048]{1,0:T(8,128)S(1)}, u32[]{:S(2)}, u32[]{:S(2)}) %collective-permute-start.4) | collective-permute-done | bytes 65568 | tf_op jit(solution)/shard_map/ppermute | solution.py:41
  93.7 1.3 collective-permute-start.5
  95.0 3.4 %collective-permute-done.5 = f32[8,2048]{1,0:T(8,128)S(1)} collective-permute-done((f32[8,2048]{1,0:T(8,128)S(1)}, f32[8,2048]{1,0:T(8,128)S(1)}, u32[]{:S(2)}, u32[]{:S(2)}) %collective-permute-start.5) | collective-permute-done | bytes 65568 | tf_op jit(solution)/shard_map/ppermute | solution.py:41
  98.4 0.0 copy-done
  98.4 2.3 %fusion = f32[8,2048]{1,0:T(8,128)S(1)} fusion(bf16[1,512,2048]{2,1,0:T(8,128)(2,1)S(1)} %copy-done, bf16[1,2048,512]{2,1,0:T(8,128)(2,1)} %param.8, f32[8,2048]{1,0:T(8,128)S(1)} %add.43, f32[8,2048]{1,0:T(8,128)S(1)} %collective-permute-done.5), kind=kOutput, calls=%fused_computation.3 | convolution fusion | flops 33624064 | bytes 4390912 | tf_op jit(solution)/shard_map/dot_general | solution.py:81
  100.8 0.2 collective-permute-start.6
  101.0 3.1 %collective-permute-done.6 = f32[8,2048]{1,0:T(8,128)S(1)} collective-permute-done((f32[8,2048]{1,0:T(8,128)S(1)}, f32[8,2048]{1,0:T(8,128)S(1)}, u32[]{:S(2)}, u32[]{:S(2)}) %collective-permute-start.6) | collective-permute-done | bytes 65568 | tf_op jit(solution)/shard_map/ppermute | solution.py:41
  104.1 0.2 collective-permute-start.7
  104.2 4.4 %collective-permute-done.7 = f32[8,2048]{1,0:T(8,128)S(1)} collective-permute-done((f32[8,2048]{1,0:T(8,128)S(1)}, f32[8,2048]{1,0:T(8,128)S(1)}, u32[]{:S(2)}, u32[]{:S(2)}) %collective-permute-start.7) | collective-permute-done | bytes 65568 | tf_op jit(solution)/shard_map/ppermute | solution.py:41
  108.6 1.1 collective-permute-start.8
  109.7 6.6 %collective-permute-done.8 = f32[8,2048]{1,0:T(8,128)S(1)} collective-permute-done((f32[8,2048]{1,0:T(8,128)S(1)}, f32[8,2048]{1,0:T(8,128)S(1)}, u32[]{:S(2)}, u32[]{:S(2)}) %collective-permute-start.8) | collective-permute-done | bytes 65568 | tf_op jit(solution)/shard_map/ppermute | solution.py:41
  116.3 1.2 collective-permute-start.9
  117.5 3.6 %collective-permute-done.9 = f32[8,2048]{1,0:T(8,128)S(1)} collective-permute-done((f32[8,2048]{1,0:T(8,128)S(1)}, f32[8,2048]{1,0:T(8,128)S(1)}, u32[]{:S(2)}, u32[]{:S(2)}) %collective-permute-start.9) | collective-permute-done | bytes 65568 | tf_op jit(solution)/shard_map/ppermute | solution.py:41
  121.1 22.9 %all_to_all.25 = bf16[16,8,2048]{2,1,0:T(8,128)(2,1)S(1)} all-to-all(bf16[16,8,2048]{2,1,0:T(8,128)(2,1)S(1)} %stack.2), channel_id=1, replica_groups=mesh['pos'=16,'exp'=16] {'exp'}, dimensions={0} | all-to-all | bytes 1048576 | tf_op jit(solution)/shard_map/all_to_all | solution.py:12
  143.9 3.3 %convolution_convert_fusion = bf16[1024,2048]{1,0:T(8,128)(2,1)} fusion(bf16[16,8,2048]{2,1,0:T(8,128)(2,1)S(1)} %all_to_all.25, f32[1024,128]{1,0:T(8,128)S(1)} %get-tuple-element.13, f32[1024]{0:T(1024)S(1)} %get-tuple-element.5, f32[1024]{0:T(1024)S(1)} %get-tuple-element.7), kind=kOutput, calls=%fused_computation.1 | convolution fusion | flops 539361280 | bytes 5251072 | tf_op jit(solution)/shard_map/dot_general | solution.py:86
  147.2 7.2 %reshape.36 = bf16[256,4,2048]{2,1,0:T(4,128)(2,1)} reshape(bf16[1024,2048]{1,0:T(8,128)(2,1)} %convolution_convert_fusion) | data formatting | bytes 8388608 | tf_op jit(solution)/shard_map/reshape | solution.py:87
  (11 shorter events, 0.2 us)
Async XLA Ops:
  0.0 98.4 %copy-start = (bf16[1,512,2048]{2,1,0:T(8,128)(2,1)S(1)}, bf16[1,512,2048]{2,1,0:T(8,128)(2,1)}, u32[]{:S(2)}) copy-start(bf16[1,512,2048]{2,1,0:T(8,128)(2,1)} %param.9) | copy-start | bytes 6291460
  0.9 14.0 %collective-permute-start.1 = (bf16[1,4,256]{2,1,0:T(4,128)(2,1)S(1)}, bf16[1,4,256]{2,1,0:T(4,128)(2,1)S(1)}, u32[]{:S(2)}, u32[]{:S(2)}) collective-permute-start(bf16[1,4,256]{2,1,0:T(4,128)(2,1)S(1)} %get-tuple-element.11), channel_id=1, source_target_pairs={{1,0},{2,1},{3,2},{4,3},{5,4},{6,5},{7,6},{8,7},{9,8},{10,9},{11,1... | collective-permute-start | bytes 6152 | tf_op jit(solution)/shard_map/ppermute | solution.py:31
  6.0 8.9 %collective-permute-start = (bf16[1,4,256]{2,1,0:T(4,128)(2,1)S(1)}, bf16[1,4,256]{2,1,0:T(4,128)(2,1)S(1)}, u32[]{:S(2)}, u32[]{:S(2)}) collective-permute-start(bf16[1,4,256]{2,1,0:T(4,128)(2,1)S(1)} %get-tuple-element.12), channel_id=1, source_target_pairs={{0,1},{1,2},{2,3},{3,4},{4,5},{5,6},{6,7},{7,8},{8,9},{9,10},{10,1... | collective-permute-start | bytes 6152 | tf_op jit(solution)/shard_map/ppermute | solution.py:30
  9.1 5.8 %copy-start.2 = (bf16[256,4,256]{2,1,0:T(4,128)(2,1)S(1)}, bf16[256,4,256]{2,1,0:T(4,128)(2,1)}, u32[]{:S(2)}) copy-start(bf16[256,4,256]{2,1,0:T(4,128)(2,1)} %param.5) | copy-start | bytes 1572868
  17.3 3.7 %copy-start.1 = (f32[1024,2048]{1,0:T(8,128)S(1)}, f32[1024,2048]{1,0:T(8,128)}, u32[]{:S(2)}) copy-start(f32[1024,2048]{1,0:T(8,128)} %fusion.8) | copy-start | bytes 25165828
  21.0 2.7 %copy-start.3 = (bf16[2048,128]{1,0:T(8,128)(2,1)S(1)}, bf16[2048,128]{1,0:T(8,128)(2,1)}, u32[]{:S(2)}) copy-start(bf16[2048,128]{1,0:T(8,128)(2,1)} %param.7) | copy-start | bytes 1572868
  78.4 3.2 %collective-permute-start.2 = (f32[8,2048]{1,0:T(8,128)S(1)}, f32[8,2048]{1,0:T(8,128)S(1)}, u32[]{:S(2)}, u32[]{:S(2)}) collective-permute-start(f32[8,2048]{1,0:T(8,128)S(1)} %reduce_sum.39), channel_id=1, source_target_pairs={{0,16},{16,0},{32,48},{48,32},{64,80},{80,64},{96,112},{112,96},{1... | collective-permute-start | bytes 196616 | tf_op jit(solution)/shard_map/ppermute | solution.py:41
  81.6 4.8 %collective-permute-start.3 = (f32[8,2048]{1,0:T(8,128)S(1)}, f32[8,2048]{1,0:T(8,128)S(1)}, u32[]{:S(2)}, u32[]{:S(2)}) collective-permute-start(f32[8,2048]{1,0:T(8,128)S(1)} %add.41), channel_id=1, source_target_pairs={{0,32},{16,48},{32,0},{48,16},{64,96},{80,112},{96,64},{112,80},{1... | collective-permute-start | bytes 196616 | tf_op jit(solution)/shard_map/ppermute | solution.py:41
  86.4 7.3 %collective-permute-start.4 = (f32[8,2048]{1,0:T(8,128)S(1)}, f32[8,2048]{1,0:T(8,128)S(1)}, u32[]{:S(2)}, u32[]{:S(2)}) collective-permute-start(f32[8,2048]{1,0:T(8,128)S(1)} %add.42), channel_id=1, source_target_pairs={{0,64},{16,80},{32,96},{48,112},{64,0},{80,16},{96,32},{112,48},{1... | collective-permute-start | bytes 196616 | tf_op jit(solution)/shard_map/ppermute | solution.py:41
  93.7 4.7 %collective-permute-start.5 = (f32[8,2048]{1,0:T(8,128)S(1)}, f32[8,2048]{1,0:T(8,128)S(1)}, u32[]{:S(2)}, u32[]{:S(2)}) collective-permute-start(f32[8,2048]{1,0:T(8,128)S(1)} %add.43), channel_id=1, source_target_pairs={{0,128},{16,144},{32,160},{48,176},{64,192},{80,208},{96,224},{112... | collective-permute-start | bytes 196616 | tf_op jit(solution)/shard_map/ppermute | solution.py:41
  100.8 3.3 %collective-permute-start.6 = (f32[8,2048]{1,0:T(8,128)S(1)}, f32[8,2048]{1,0:T(8,128)S(1)}, u32[]{:S(2)}, u32[]{:S(2)}) collective-permute-start(f32[8,2048]{1,0:T(8,128)S(1)} %fusion), channel_id=1, source_target_pairs={{0,16},{16,0},{32,48},{48,32},{64,80},{80,64},{96,112},{112,96},{1... | collective-permute-start | bytes 196616 | tf_op jit(solution)/shard_map/ppermute | solution.py:41
  104.1 4.5 %collective-permute-start.7 = (f32[8,2048]{1,0:T(8,128)S(1)}, f32[8,2048]{1,0:T(8,128)S(1)}, u32[]{:S(2)}, u32[]{:S(2)}) collective-permute-start(f32[8,2048]{1,0:T(8,128)S(1)} %add.48), channel_id=1, source_target_pairs={{0,32},{16,48},{32,0},{48,16},{64,96},{80,112},{96,64},{112,80},{1... | collective-permute-start | bytes 196616 | tf_op jit(solution)/shard_map/ppermute | solution.py:41
  108.6 7.7 %collective-permute-start.8 = (f32[8,2048]{1,0:T(8,128)S(1)}, f32[8,2048]{1,0:T(8,128)S(1)}, u32[]{:S(2)}, u32[]{:S(2)}) collective-permute-start(f32[8,2048]{1,0:T(8,128)S(1)} %add.49), channel_id=1, source_target_pairs={{0,64},{16,80},{32,96},{48,112},{64,0},{80,16},{96,32},{112,48},{1... | collective-permute-start | bytes 196616 | tf_op jit(solution)/shard_map/ppermute | solution.py:41
  116.3 4.7 %collective-permute-start.9 = (f32[8,2048]{1,0:T(8,128)S(1)}, f32[8,2048]{1,0:T(8,128)S(1)}, u32[]{:S(2)}, u32[]{:S(2)}) collective-permute-start(f32[8,2048]{1,0:T(8,128)S(1)} %add.50), channel_id=1, source_target_pairs={{0,128},{16,144},{32,160},{48,176},{64,192},{80,208},{96,224},{112... | collective-permute-start | bytes 196616 | tf_op jit(solution)/shard_map/ppermute | solution.py:41
